TPU v7x, 512 devices: a whole 4x4x16 slice. The times are simulated.
512 devices in a mesh: pole: 2 (over core), prow: 16 (over z), pcol: 16 (over x, y).
Axes of the slice: x: 4, y: 4, z: 16, core: 2. Of those that a mesh axis runs over, the one named last changes fastest.
Arguments:
- inverse_trailing: float32 [32768, 16384], P(('pole', 'prow'), 'pcol'), parts along dimension 0, may hold values from -6 to 6
- factor_blocks: float32 [6, 4096, 256], P('pole', 'prow'), parts along dimension 0, may hold values from -0.09375 to 0.09375
- diag_pivots: float32 [256, 6, 256], P('pcol', 'pole'), parts along dimension 1, may hold values from -6 to 6
- structure: int32 [3, 16], replicated, may hold values from 0 to 63, as said below
- owner_map: int32 [64], replicated, may hold values from 0 to 63, each once
Outputs:
- row_inverse: float32 [256, 6, 16384], P('pcol', 'pole', 'prow'), parts along dimension 1
- diag_inverse: float32 [256, 6, 256], P('pcol', 'pole'), parts along dimension 1
There are 2 independent parts, one for each index of `pole`. A program takes and returns all parts, laid end to end along the dimension named above; an argument that names none is the same for every part. Nothing has to cross between parts.
Inputs may be any that keep to these rules, and one draw needn't show every extreme that they name: `structure`: each row lists 16 distinct logical ancestor blocks.
All inputs are finite; a program needn't handle non-finite values.
Results may differ from a plain program's by a relative error of at most 0.0001.
Values sent between devices are 32-bit elements; how exact they have to be, the bound alone decides.
No kernel may reach another device: no remote copies, remote signals or barrier semaphores. Data moves between devices by JAX's collectives and lax.ppermute only.
A program may use at most 64 MiB of HBM per device.

v0:
```python
import functools

import jax
import jax.numpy as jnp
from jax import lax
from jax.sharding import PartitionSpec as P


def diag_product(values, factor):
    return jnp.einsum("awj,wjb->awb", values, factor, precision=lax.Precision.HIGHEST)


def slot_lookup(positions, slots):
    match = positions[:, None, :] == slots[None, :, None]
    return jnp.argmax(match, axis=2), jnp.any(match, axis=2)


PACKED = (6, 8, 12)


def pack_order(present, size):
    rank = jnp.cumsum(present.astype(jnp.int32), axis=1) - 1
    target = jnp.arange(size, dtype=jnp.int32)
    hit = present[:, None, :] & (rank[:, None, :] == target[None, :, None])
    return jnp.argmax(hit, axis=2).astype(jnp.int32), jnp.any(hit, axis=2)


def make_shards(prow_size, pcol_size):
    def shards(inverse_trailing, factor_blocks, diag_pivots, structure, owner_map):
        width = factor_blocks.shape[2]
        window = factor_blocks.shape[0]
        local_rows = factor_blocks.shape[1]
        owned = inverse_trailing.shape[0] // width
        row_index = lax.axis_index("prow")
        col_index = lax.axis_index("pcol")
        positions = jnp.take(owner_map, structure, axis=0)
        slots = jnp.arange(owned, dtype=jnp.int32)
        segment = local_rows // pcol_size
        mine = lax.dynamic_slice_in_dim(factor_blocks, col_index * segment, segment, axis=1)
        pieces = lax.all_gather(mine, "prow", axis=1, tiled=True)
        count = pieces.shape[1] // segment
        pieces = pieces.reshape(window, count, segment, width)
        windows = jnp.arange(window)
        flat_slots = window * owned
        dest_slots = jnp.arange(pcol_size, dtype=jnp.int32)[:, None] * owned + slots[None, :]
        dest_index, dest_present = jax.vmap(lambda s: slot_lookup(positions, s))(dest_slots)
        dest_index = dest_index.reshape(pcol_size, flat_slots)
        dest_present = dest_present.reshape(pcol_size, flat_slots)
        row_index_map, in_rows = slot_lookup(positions, row_index * owned + slots)
        row_piece = pieces[windows[:, None], row_index_map]
        row_piece = jnp.where(in_rows[..., None, None], row_piece, 0.0)
        row_factor = lax.all_gather(row_piece, "pcol", axis=2, tiled=True)
        row_factor = row_factor.reshape(window, owned * width, width)
        needed = jnp.max(jnp.sum(dest_present.astype(jnp.int32), axis=1))
        branch = jnp.sum((needed > jnp.array(PACKED[:-1], jnp.int32)).astype(jnp.int32))

        def route(size, pieces):
            send_slot, send_valid = pack_order(dest_present, size)
            send_w = send_slot // owned
            send_j = jnp.take_along_axis(dest_index, send_slot, axis=1)
            send = pieces[send_w, send_j]
            send = jnp.where(send_valid[..., None, None], send, 0.0)
            received = lax.all_to_all(send, "pcol", 0, 0, tiled=True)
            blocks = jnp.transpose(received, (1, 0, 2, 3)).reshape(size, local_rows, width)
            mine = dest_present[col_index]
            rank = jnp.clip(jnp.cumsum(mine.astype(jnp.int32)) - 1, 0, size - 1)
            return jnp.where(mine[:, None, None], blocks[rank], 0.0)

        def reduce_rows(size, partial):
            pair_slot, _ = pack_order(listed[None, :], size)
            chosen = jnp.take(partial, pair_slot[0], axis=1)
            share = chosen.shape[0] // pcol_size
            chosen = chosen.reshape((pcol_size, share) + chosen.shape[1:])
            summed = jnp.sum(lax.all_to_all(chosen, "pcol", 0, 0, tiled=True), axis=0)
            pair_rank = jnp.clip(jnp.cumsum(listed.astype(jnp.int32)) - 1, 0, size - 1)
            return jnp.where(listed[None, :, None], -jnp.take(summed, pair_rank, axis=1), 0.0)

        listed = in_rows.reshape(flat_slots)
        col_factor = lax.switch(branch, [functools.partial(route, size) for size in PACKED], pieces)
        col_factor = col_factor.reshape(window, owned * local_rows, width)
        partial = jnp.einsum("wja,ij->awi", col_factor, inverse_trailing, precision=lax.Precision.HIGHEST)
        partial = partial.reshape(partial.shape[0], flat_slots, width)
        rows = lax.switch(branch, [functools.partial(reduce_rows, size) for size in PACKED], partial)
        row_inverse = rows.reshape(rows.shape[0], window, owned * width)
        local_diag = diag_product(row_inverse, row_factor)
        gathered = lax.all_gather(local_diag, "prow", axis=0, tiled=False)
        total_diag = jnp.sum(gathered, axis=0)
        diag_inverse = diag_pivots - total_diag
        return (row_inverse, diag_inverse)

    return shards


def solution(mesh):
    in_specs = (
        P(("pole", "prow"), "pcol"),
        P("pole", "prow", None),
        P("pcol", "pole", None),
        P(),
        P(),
    )
    out_specs = (P("pcol", "pole", "prow"), P("pcol", "pole", None))
    shards = make_shards(mesh.shape["prow"], mesh.shape["pcol"])
    return jax.shard_map(shards, mesh=mesh, in_specs=in_specs, out_specs=out_specs, check_vma=False)
```

profile of v0, /device:TPU:32, one launch (start us, length us, event | category | flops | bytes accessed | tf_op | source)
XLA Modules:
  0.0 206.0 jit_solution(17449391272853971554)
XLA Ops:
  8.1 1.4 gather_fusion.15
  11.3 37.7 %all_gather.12 = f32[3,256,256]{2,1,0:T(8,128)S(1)} all-gather(f32[3,16,256]{2,1,0:T(8,128)S(1)} %constant_dynamic-slice_fusion), channel_id=1, replica_groups=mesh['pole'=2,'prow'=16,'pcol'=16] {'prow'}, dimensions={1}, use_global_device_ids=true | all-gather | bytes 835584 | tf_op jit(solution)/shard_map/all_gather | solution.py:40
  50.8 1.2 compare_reduce_fusion
  52.7 1.3 fusion.49
  54.6 46.4 %conditional.2 = (f32[3,1024,256]{2,1,0:T(8,128)}) conditional(s32[]{:T(128)} %clamp.64, (pred[16,3,4]{0,2,1:T(4,128)(4,1)S(1)}, s32[]{:T(128)}, s32[16,3,4]{0,2,1:T(4,128)S(1)}, f32[3,16,16,256]{3,2,1,0:T(8,128)S(1)}) %tuple.104, (pred[16,3,4]{0,2,1:T(4,128)(4,1)S(1)}, s32[]{:T(128)}, s32[16,3,4]{0,2,1:T(4,128)S(1)}, ...), branch_computations={%region_6.11_spmd, %region_11.16_spmd, %region_16.21_spmd} | conditional | flops 1610383 | bytes 40940528 | solution.py:79
  55.5 1.3 gather_fusion.5
  57.2 1.1 gather_fusion.3
  58.3 1.6 broadcast_select_fusion.1
  59.9 7.0 %all-to-all-start.1 = ((f32[16,8,16,256]{3,2,1,0:T(8,128)}), f32[16,8,16,256]{3,2,1,0:T(8,128)S(1)}, u32[]{:S(2)}, u32[]{:S(2)}) async-start(f32[16,8,16,256]{3,2,1,0:T(8,128)} %broadcast_select_fusion.1), calls=%async_computation.1 | async-start | bytes 4194304 | tf_op jit(solution)/shard_map/cond/branch_1_fun/all_to_all | solution.py:63
  67.7 24.3 %all-to-all-done.1 = f32[16,8,16,256]{3,2,1,0:T(8,128)S(1)} async-done(((f32[16,8,16,256]{3,2,1,0:T(8,128)}), f32[16,8,16,256]{3,2,1,0:T(8,128)S(1)}, u32[]{:S(2)}, u32[]{:S(2)}) %all-to-all-start.1) | async-done | bytes 2097184 | tf_op jit(solution)/shard_map/cond/branch_1_fun/all_to_all | solution.py:63
  92.0 1.4 copy-done.2
  93.4 1.8 copy.231
  95.2 2.5 %gather_fusion.4 = f32[12,256,256]{2,1,0:T(8,128)} fusion(f32[8,256,256]{2,1,0:T(8,128)S(1)} %bitcast.147, s32[1024]{0:T(1024)S(1)} %pad_clamp_fusion.1), kind=kCustom, calls=%fused_computation.4 | custom fusion | bytes 6291504 | tf_op jit(solution)/shard_map/cond/branch_1_fun/gather | solution.py:67
  97.6 3.4 %bitcast_select_fusion.1 = f32[3,1024,256]{2,1,0:T(8,128)} fusion(pred[3,1024]{1,0:T(4,128)(4,1)S(1)} %bitcast.176, f32[3,1024,256]{2,1,0:T(8,128)} %bitcast.155), kind=kLoop, calls=%fused_computation.46 | loop fusion | flops 786432 | bytes 6294528 | tf_op jit(solution)/shard_map/cond/branch_1_fun/jit(_where)/select_n | solution.py:67
  101.0 22.8 %fusion.42 = f32[256,3,1024]{2,0,1:T(8,128)S(1)} fusion(f32[3,1024,256]{2,1,0:T(8,128)} %get-tuple-element.203, f32[1024,1024]{1,0:T(8,128)} %param.12), kind=kOutput, calls=%fused_computation.162 | convolution fusion | flops 9663676416 | bytes 10485760 | tf_op jit(solution)/shard_map/wja,ij->awi/dot_general | solution.py:81
  123.8 37.4 %conditional.3 = (f32[16,3,1024]{2,0,1:T(8,128)S(1)}) conditional(s32[]{:T(128)} %clamp.64, (pred[3,4]{1,0:T(4,128)(4,1)S(1)}, f32[256,3,1024]{2,0,1:T(8,128)S(1)}) %tuple.49, (pred[3,4]{1,0:T(4,128)(4,1)S(1)}, f32[256,3,1024]{2,0,1:T(8,128)S(1)}) %tuple.49, (pred[3,4]{1,0:T(4,128)(4,1)S(1)}, ...), branch_computations={%region_21.26_spmd, %region_26.31_spmd, %region_31.36_spmd} | conditional | flops 1674812 | bytes 39945468 | solution.py:83
  125.1 2.4 %copy.250 = f32[256,3,1024]{0,2,1:T(8,128)} copy(f32[256,3,1024]{2,0,1:T(8,128)S(1)} %get-tuple-element.185) | data formatting | bytes 6291456 | tf_op jit(solution)/shard_map
  127.5 2.4 %copy.242 = f32[256,12,256]{2,0,1:T(8,128)S(1)} copy(f32[256,12,256]{0,2,1:T(8,128)} %bitcast.152) | data formatting | bytes 6291456 | tf_op jit(solution)/shard_map/reshape | solution.py:82
  129.9 2.1 gather_fusion.11
  131.9 3.3 %copy_select_fusion.1 = f32[16,16,8,256]{3,1,2,0:T(8,128)} fusion(f32[16,16,8,256]{3,1,0,2:T(8,128)} %bitcast.159, pred[8]{0:T(512)(128)(4,1)S(1)} %compare_and_fusion.2), kind=kLoop, calls=%fused_computation.122 | loop fusion | flops 524288 | bytes 4194312 | tf_op jit(solution)/shard_map/cond/branch_1_fun/jit(_take)/select_n | solution.py:71
  135.3 3.9 %all-to-all-start.4 = ((f32[16,16,8,256]{3,1,2,0:T(8,128)}), f32[16,16,8,256]{3,1,2,0:T(8,128)S(1)}, u32[]{:S(2)}, u32[]{:S(2)}) async-start(f32[16,16,8,256]{3,1,2,0:T(8,128)} %copy_select_fusion.1), calls=%async_computation.4 | async-start | bytes 4194304 | tf_op jit(solution)/shard_map/cond/branch_1_fun/all_to_all | solution.py:74
  139.5 20.5 %all-to-all-done.4 = f32[16,16,8,256]{3,1,2,0:T(8,128)S(1)} async-done(((f32[16,16,8,256]{3,1,2,0:T(8,128)}), f32[16,16,8,256]{3,1,2,0:T(8,128)S(1)}, u32[]{:S(2)}, u32[]{:S(2)}) %all-to-all-start.4) | async-done | bytes 2097184 | tf_op jit(solution)/shard_map/cond/branch_1_fun/all_to_all | solution.py:74
  161.2 3.7 %convolution_bitcast_fusion = f32[16,3,256]{2,0,1:T(8,128)S(1)} fusion(f32[3,1024,256]{2,1,0:T(8,128)} %bitcast.163, f32[16,3,1024]{2,0,1:T(8,128)S(1)} %get-tuple-element.190), kind=kOutput, calls=%fused_computation.163 | convolution fusion | flops 150994944 | bytes 3391488 | tf_op jit(solution)/shard_map/awj,wjb->awb/dot_general | solution.py:10
  164.9 33.5 %all-gather = f32[256,3,256]{2,0,1:T(8,128)S(1)} all-gather(f32[16,3,256]{2,0,1:T(8,128)S(1)} %convolution_bitcast_fusion), channel_id=2, replica_groups=mesh['pole'=2,'prow'=16,'pcol'=16] {'prow'}, dimensions={0}, use_global_device_ids=true | all-gather | bytes 835584 | tf_op jit(solution)/shard_map/all_gather | solution.py:86
  (80 shorter events, 10.4 us)
Async XLA Ops:
  7.2 4.1 %copy-start = (f32[3,256,256]{2,1,0:T(8,128)S(1)}, f32[3,256,256]{2,1,0:T(8,128)}, u32[]{:S(2)}) copy-start(f32[3,256,256]{2,1,0:T(8,128)} %param.13) | copy-start | bytes 2359300
  7.2 45.5 %copy-start.5 = (s32[2]{0:T(128)S(1)}, s32[2]{0:T(128)}, u32[]{:S(2)}) copy-start(s32[2]{0:T(128)} %constant.361.clone) | copy-start | bytes 28
  7.2 154.0 %all-gather.3.cloned.1.call-start = ((), (), s32[]{:S(2)}) async-start(), calls=%async_computation.6 | async-start | bytes 3342336 | tf_op jit(solution)/shard_map/all_gather | solution.py:52
  59.9 32.1 %all-to-all-start.1 = ((f32[16,8,16,256]{3,2,1,0:T(8,128)}), f32[16,8,16,256]{3,2,1,0:T(8,128)S(1)}, u32[]{:S(2)}, u32[]{:S(2)}) async-start(f32[16,8,16,256]{3,2,1,0:T(8,128)} %broadcast_select_fusion.1), calls=%async_computation.1 | async-start | bytes 4194304 | tf_op jit(solution)/shard_map/cond/branch_1_fun/all_to_all | solution.py:63
  92.0 1.4 copy-start.2
  135.3 24.7 %all-to-all-start.4 = ((f32[16,16,8,256]{3,1,2,0:T(8,128)}), f32[16,16,8,256]{3,1,2,0:T(8,128)S(1)}, u32[]{:S(2)}, u32[]{:S(2)}) async-start(f32[16,16,8,256]{3,1,2,0:T(8,128)} %copy_select_fusion.1), calls=%async_computation.4 | async-start | bytes 4194304 | tf_op jit(solution)/shard_map/cond/branch_1_fun/all_to_all | solution.py:74
  161.2 38.0 %copy-start.3 = (f32[16,3,1024]{2,0,1:T(8,128)}, f32[16,3,1024]{2,0,1:T(8,128)S(1)}, u32[]{:S(2)}) copy-start(f32[16,3,1024]{2,0,1:T(8,128)S(1)} %get-tuple-element.190) | copy-start | bytes 589828
  161.2 37.3 %copy-start.4 = (f32[16,3,256]{2,0,1:T(8,128)S(1)}, f32[16,3,256]{2,0,1:T(8,128)}, u32[]{:S(2)}) copy-start(f32[16,3,256]{2,0,1:T(8,128)} %param.14) | copy-start | bytes 147460
  161.2 38.0 %copy-start.1 = (f32[3,256,256]{2,1,0:T(8,128)S(1)}, f32[3,256,256]{2,1,0:T(8,128)}, u32[]{:S(2)}) copy-start(f32[3,256,256]{2,1,0:T(8,128)} %param.13) | copy-start | bytes 2359300
Sparse Core Ops, SparseCore 0:
  50.6 70.2 all-gather.2
where the time goes:
time: 206 us
  blocking collectives  71.2 us (35%)
  waiting for transfers between devices  44.8 us (22%)
  matrix products  26.5 us (13%)
  local copies, waits for them, and re-layouts  19.5 us (9%)
  other arithmetic  17.8 us (9%)
  between operations  14.8 us (7%)
  starting transfers between devices  11 us (5%)
    all_gather x1, blocking collectives, shards(): pieces = lax.all_gather(mine, 'prow', axis=1, tiled=True)  37.7 us
    all_gather x1, blocking collectives, shards(): gathered = lax.all_gather(local_diag, 'prow', axis=0, tiled=False)  33.5 us
    all_to_all x1, waiting for transfers between devices, route(): received = lax.all_to_all(send, 'pcol', 0, 0, tiled=True)  24.3 us
    dot_general x1, matrix products, shards(): jnp.einsum('wja,ij->awi', col_factor, inverse_trailing, precision=lax.Pre...  22.8 us
    all_to_all x1, waiting for transfers between devices, reduce_rows(): summed = jnp.sum(lax.all_to_all(chosen, 'pcol', 0, 0, tiled=True), axis=0)  20.5 us
    all_to_all x1, starting transfers between devices, route(): received = lax.all_to_all(send, 'pcol', 0, 0, tiled=True)  7.03 us
  transfers between devices with their start and end apart: 3, of which 2 were waited for; matrix products, arithmetic and copies ran while one was open for 25% of the time, Pallas kernels for 0%

commit v1 on v0

--- a/solution.py
+++ b/solution.py
@@ -68,18 +68,20 @@
 
         def reduce_rows(size, partial):
             pair_slot, _ = pack_order(listed[None, :], size)
-            chosen = jnp.take(partial, pair_slot[0], axis=1)
-            share = chosen.shape[0] // pcol_size
-            chosen = chosen.reshape((pcol_size, share) + chosen.shape[1:])
-            summed = jnp.sum(lax.all_to_all(chosen, "pcol", 0, 0, tiled=True), axis=0)
+            pair_slot = pair_slot[0]
+            chosen = partial[pair_slot // owned, :, pair_slot % owned]
+            share = chosen.shape[1] // pcol_size
+            chosen = chosen.reshape((size, pcol_size, share) + chosen.shape[2:])
+            summed = jnp.sum(lax.all_to_all(chosen, "pcol", 1, 1, tiled=True), axis=1)
             pair_rank = jnp.clip(jnp.cumsum(listed.astype(jnp.int32)) - 1, 0, size - 1)
-            return jnp.where(listed[None, :, None], -jnp.take(summed, pair_rank, axis=1), 0.0)
+            rows = jnp.where(listed[:, None, None], -jnp.take(summed, pair_rank, axis=0), 0.0)
+            return jnp.transpose(rows, (1, 0, 2))
 
         listed = in_rows.reshape(flat_slots)
         col_factor = lax.switch(branch, [functools.partial(route, size) for size in PACKED], pieces)
         col_factor = col_factor.reshape(window, owned * local_rows, width)
-        partial = jnp.einsum("wja,ij->awi", col_factor, inverse_trailing, precision=lax.Precision.HIGHEST)
-        partial = partial.reshape(partial.shape[0], flat_slots, width)
+        partial = jnp.einsum("wja,ij->wai", col_factor, inverse_trailing, precision=lax.Precision.HIGHEST)
+        partial = partial.reshape(window, partial.shape[1], owned, width)
         rows = lax.switch(branch, [functools.partial(reduce_rows, size) for size in PACKED], partial)
         row_inverse = rows.reshape(rows.shape[0], window, owned * width)
         local_diag = diag_product(row_inverse, row_factor)

time: 206 us -> 187 us (0.908)
  waiting for transfers between devices: 44.8 us -> 33.3 us
  local copies, waits for them, and re-layouts: 19.5 us -> 14.2 us
  other arithmetic: 17.8 us -> 14.9 us
    all_to_all x1, waiting for transfers between devices: 24.3 us -> 17.1 us  [route(): received = lax.all_to_all(send, 'pcol', 0, 0, tiled=True)]
    all_to_all x1, waiting for transfers between devices: 20.5 us -> 16.2 us  [reduce_rows(): summed = jnp.sum(lax.all_to_all(chosen, 'pcol', 1, 1, tiled=True), axis=1)]
    select_n x3 -> x2, other arithmetic: 3.43 us -> 0.1 us  [the longest x1 0.09 us: reduce_rows(): jnp.where(listed[:, None, None], -jnp.take(summed, pair_rank, axis=0), 0.0)]
    another operation x1 -> x0, local copies, waits for them, and re-layouts: 2.4 us -> none
  transfers between devices with their start and end apart: 3 -> 3, of which waited for: 2 -> 2; matrix products, arithmetic and copies ran while one was open for 25% -> 24% of each run, Pallas kernels for 0% -> 0%
where the time goes in v1:
time: 187 us; the launch traced here: 186 us
  blocking collectives  71 us (38%)
  waiting for transfers between devices  33.3 us (18%)
  matrix products  26.1 us (14%)
  other arithmetic  14.9 us (8%)
  between operations  14.8 us (8%)
  local copies, waits for them, and re-layouts  14.2 us (8%)
  starting transfers between devices  11.8 us (6%)
    all_gather x1, blocking collectives, shards(): pieces = lax.all_gather(mine, 'prow', axis=1, tiled=True)  37.7 us
    all_gather x1, blocking collectives, shards(): gathered = lax.all_gather(local_diag, 'prow', axis=0, tiled=False)  33.3 us
    dot_general x1, matrix products, shards(): jnp.einsum('wja,ij->wai', col_factor, inverse_trailing, precision=lax.Pre...  22.3 us
    all_to_all x1, waiting for transfers between devices, route(): received = lax.all_to_all(send, 'pcol', 0, 0, tiled=True)  17.1 us
    all_to_all x1, waiting for transfers between devices, reduce_rows(): summed = jnp.sum(lax.all_to_all(chosen, 'pcol', 1, 1, tiled=True), axis=1)  16.2 us
    all_to_all x1, starting transfers between devices, route(): received = lax.all_to_all(send, 'pcol', 0, 0, tiled=True)  7.03 us
    all_to_all x1, starting transfers between devices, reduce_rows(): summed = jnp.sum(lax.all_to_all(chosen, 'pcol', 1, 1, tiled=True), axis=1)  4.78 us
  transfers between devices with their start and end apart: 3, of which 2 were waited for; matrix products, arithmetic and copies ran while one was open for 24% of the time, Pallas kernels for 0%

profile of v1, /device:TPU:32, one launch (start us, length us, event | category | flops | bytes accessed | tf_op | source)
XLA Modules:
  0.0 186.4 jit_solution(11930366651583640431)
XLA Ops:
  7.2 0.7 compare_select_fusion.31
  8.1 1.4 gather_fusion.15
  11.3 37.7 %all_gather.12 = f32[3,256,256]{2,1,0:T(8,128)S(1)} all-gather(f32[3,16,256]{2,1,0:T(8,128)S(1)} %constant_dynamic-slice_fusion), channel_id=1, replica_groups=mesh['pole'=2,'prow'=16,'pcol'=16] {'prow'}, dimensions={1}, use_global_device_ids=true | all-gather | bytes 835584 | tf_op jit(solution)/shard_map/all_gather | solution.py:40
  49.6 0.8 broadcast_select_fusion.3
  50.8 1.2 compare_reduce_fusion
  52.7 1.3 fusion.61
  54.6 36.7 %conditional.2 = (f32[3,1024,256]{2,1,0:T(8,128)}) conditional(s32[]{:T(128)} %clamp.61, (pred[16,3,4]{0,2,1:T(4,128)(4,1)S(1)}, s32[]{:T(128)}, s32[16,3,4]{0,2,1:T(4,128)S(1)}, f32[3,16,16,256]{3,2,1,0:T(8,128)S(1)}) %tuple.86, (pred[16,3,4]{0,2,1:T(4,128)(4,1)S(1)}, s32[]{:T(128)}, s32[16,3,4]{0,2,1:T(4,128)S(1)}, ...), branch_computations={%region_6.11_spmd, %region_11.16_spmd, %region_16.21_spmd} | conditional | flops 1610383 | bytes 40940528 | solution.py:81
  54.9 0.9 iota_reduce_fusion.1
  56.1 1.3 gather_fusion.4
  57.9 1.2 gather_fusion.2
  59.1 1.3 broadcast_select_fusion
  60.4 7.0 %all-to-all-start.1 = ((f32[16,6,16,256]{3,2,1,0:T(8,128)}), f32[16,6,16,256]{3,2,1,0:T(8,128)S(1)}, u32[]{:S(2)}, u32[]{:S(2)}) async-start(f32[16,6,16,256]{3,2,1,0:T(8,128)} %broadcast_select_fusion), calls=%async_computation.1 | async-start | bytes 3145728 | tf_op jit(solution)/shard_map/cond/branch_0_fun/all_to_all | solution.py:63
  68.2 17.1 %all-to-all-done.1 = f32[16,6,16,256]{3,2,1,0:T(8,128)S(1)} async-done(((f32[16,6,16,256]{3,2,1,0:T(8,128)}), f32[16,6,16,256]{3,2,1,0:T(8,128)S(1)}, u32[]{:S(2)}, u32[]{:S(2)}) %all-to-all-start.1) | async-done | bytes 1572896 | tf_op jit(solution)/shard_map/cond/branch_0_fun/all_to_all | solution.py:63
  85.5 2.5 %gather_fusion.3 = f32[12,256,256]{2,1,0:T(8,128)} fusion(f32[6,256,256]{2,1,0:T(8,128)S(1)} %bitcast.165, s32[1024]{0:T(1024)S(1)} %pad_clamp_fusion.1), kind=kCustom, calls=%fused_computation.1 | custom fusion | bytes 6291504 | tf_op jit(solution)/shard_map/cond/branch_0_fun/gather | solution.py:67
  87.9 3.4 %bitcast_select_fusion = f32[3,1024,256]{2,1,0:T(8,128)} fusion(pred[3,1024]{1,0:T(4,128)(4,1)S(1)} %bitcast.184, f32[3,1024,256]{2,1,0:T(8,128)} %bitcast.171), kind=kLoop, calls=%fused_computation.42 | loop fusion | flops 786432 | bytes 6294528 | tf_op jit(solution)/shard_map/cond/branch_0_fun/jit(_where)/select_n | solution.py:67
  91.3 22.3 %fusion.55 = f32[3,256,4,256]{3,1,2,0:T(8,128)S(1)} fusion(f32[4,256,1024,1]{2,1,0,3:T(8,128)} %bitcast.180, f32[3,1024,256]{2,1,0:T(8,128)} %get-tuple-element.167), kind=kOutput, calls=%fused_computation.175 | convolution fusion | flops 9663676416 | bytes 10485760 | tf_op jit(solution)/shard_map/wja,ij->wai/dot_general | solution.py:83
  113.7 28.1 %conditional.3 = (f32[16,3,1024]{2,0,1:T(8,128)S(1)}) conditional(s32[]{:T(128)} %clamp.61, (pred[3,4]{1,0:T(4,128)(4,1)S(1)}, f32[3,256,4,256]{3,1,2,0:T(8,128)S(1)}) %tuple.49, (pred[3,4]{1,0:T(4,128)(4,1)S(1)}, f32[3,256,4,256]{3,1,2,0:T(8,128)S(1)}) %tuple.49, (pred[3,4]{1,0:T(4,128)(4,1)S(1)}, ...), branch_computations={%region_21.26_spmd, %region_26.31_spmd, %region_31.36_spmd} | conditional | flops 887632 | bytes 27333668 | solution.py:85
  114.0 0.9 and_reduce_fusion
  115.0 1.8 gather_fusion.11
  116.9 2.7 %copy.215 = f32[6,16,16,256]{3,2,0,1:T(8,128)} copy(f32[6,16,16,256]{3,2,1,0:T(8,128)} %bitcast.178) | data formatting | bytes 3145728 | tf_op jit(solution)/shard_map/cond/branch_0_fun/reshape | solution.py:74
  119.6 4.8 %all-to-all-start.4 = ((f32[6,16,16,256]{3,2,0,1:T(8,128)}), f32[6,16,16,256]{3,2,0,1:T(8,128)S(1)}, u32[]{:S(2)}, u32[]{:S(2)}) async-start(f32[6,16,16,256]{3,2,0,1:T(8,128)} %copy.215), calls=%async_computation.4 | async-start | bytes 3145728 | tf_op jit(solution)/shard_map/cond/branch_0_fun/all_to_all | solution.py:75
  124.4 16.2 %all-to-all-done.4 = f32[6,16,16,256]{3,2,0,1:T(8,128)S(1)} async-done(((f32[6,16,16,256]{3,2,0,1:T(8,128)}), f32[6,16,16,256]{3,2,0,1:T(8,128)S(1)}, u32[]{:S(2)}, u32[]{:S(2)}) %all-to-all-start.4) | async-done | bytes 1572896 | tf_op jit(solution)/shard_map/cond/branch_0_fun/all_to_all | solution.py:75
  141.8 3.7 %convolution_bitcast_fusion = f32[16,3,256]{2,0,1:T(8,128)S(1)} fusion(f32[3,1024,256]{2,1,0:T(8,128)} %bitcast.181, f32[16,3,1024]{2,0,1:T(8,128)S(1)} %get-tuple-element.157), kind=kOutput, calls=%fused_computation.177 | convolution fusion | flops 150994944 | bytes 3391488 | tf_op jit(solution)/shard_map/awj,wjb->awb/dot_general | solution.py:10
  145.5 33.3 %all-gather = f32[256,3,256]{2,0,1:T(8,128)S(1)} all-gather(f32[16,3,256]{2,0,1:T(8,128)S(1)} %convolution_bitcast_fusion), channel_id=2, replica_groups=mesh['pole'=2,'prow'=16,'pcol'=16] {'prow'}, dimensions={0}, use_global_device_ids=true | all-gather | bytes 835584 | tf_op jit(solution)/shard_map/all_gather | solution.py:88
  (72 shorter events, 8.0 us)
Async XLA Ops:
  7.2 4.1 %copy-start = (f32[3,256,256]{2,1,0:T(8,128)S(1)}, f32[3,256,256]{2,1,0:T(8,128)}, u32[]{:S(2)}) copy-start(f32[3,256,256]{2,1,0:T(8,128)} %param.13) | copy-start | bytes 2359300
  7.2 45.5 %copy-start.5 = (s32[2]{0:T(128)S(1)}, s32[2]{0:T(128)}, u32[]{:S(2)}) copy-start(s32[2]{0:T(128)} %constant.408.clone) | copy-start | bytes 28
  7.2 134.6 %all-gather.3.cloned.1.call-start = ((), (), s32[]{:S(2)}) async-start(), calls=%async_computation.6 | async-start | bytes 3342336 | tf_op jit(solution)/shard_map/all_gather | solution.py:52
  60.4 24.9 %all-to-all-start.1 = ((f32[16,6,16,256]{3,2,1,0:T(8,128)}), f32[16,6,16,256]{3,2,1,0:T(8,128)S(1)}, u32[]{:S(2)}, u32[]{:S(2)}) async-start(f32[16,6,16,256]{3,2,1,0:T(8,128)} %broadcast_select_fusion), calls=%async_computation.1 | async-start | bytes 3145728 | tf_op jit(solution)/shard_map/cond/branch_0_fun/all_to_all | solution.py:63
  119.6 21.0 %all-to-all-start.4 = ((f32[6,16,16,256]{3,2,0,1:T(8,128)}), f32[6,16,16,256]{3,2,0,1:T(8,128)S(1)}, u32[]{:S(2)}, u32[]{:S(2)}) async-start(f32[6,16,16,256]{3,2,0,1:T(8,128)} %copy.215), calls=%async_computation.4 | async-start | bytes 3145728 | tf_op jit(solution)/shard_map/cond/branch_0_fun/all_to_all | solution.py:75
  141.8 37.8 %copy-start.3 = (f32[16,3,1024]{2,0,1:T(8,128)}, f32[16,3,1024]{2,0,1:T(8,128)S(1)}, u32[]{:S(2)}) copy-start(f32[16,3,1024]{2,0,1:T(8,128)S(1)} %get-tuple-element.157) | copy-start | bytes 589828
  141.8 37.1 %copy-start.4 = (f32[16,3,256]{2,0,1:T(8,128)S(1)}, f32[16,3,256]{2,0,1:T(8,128)}, u32[]{:S(2)}) copy-start(f32[16,3,256]{2,0,1:T(8,128)} %param.14) | copy-start | bytes 147460
  141.8 37.8 %copy-start.1 = (f32[3,256,256]{2,1,0:T(8,128)S(1)}, f32[3,256,256]{2,1,0:T(8,128)}, u32[]{:S(2)}) copy-start(f32[3,256,256]{2,1,0:T(8,128)} %param.13) | copy-start | bytes 2359300
Sparse Core Ops, SparseCore 0:
  50.6 67.6 all-gather.2

commit v2 on v1

--- a/solution.py
+++ b/solution.py
@@ -54,10 +54,15 @@
         needed = jnp.max(jnp.sum(dest_present.astype(jnp.int32), axis=1))
         branch = jnp.sum((needed > jnp.array(PACKED[:-1], jnp.int32)).astype(jnp.int32))
 
+        full_slot, full_valid = pack_order(dest_present, flat_slots)
+        full_j = jnp.take_along_axis(dest_index, full_slot, axis=1)
+        listed = in_rows.reshape(flat_slots)
+        full_pair, _ = pack_order(listed[None, :], flat_slots)
+
         def route(size, pieces):
-            send_slot, send_valid = pack_order(dest_present, size)
+            send_slot, send_valid = full_slot[:, :size], full_valid[:, :size]
             send_w = send_slot // owned
-            send_j = jnp.take_along_axis(dest_index, send_slot, axis=1)
+            send_j = full_j[:, :size]
             send = pieces[send_w, send_j]
             send = jnp.where(send_valid[..., None, None], send, 0.0)
             received = lax.all_to_all(send, "pcol", 0, 0, tiled=True)
@@ -67,8 +72,7 @@
             return jnp.where(mine[:, None, None], blocks[rank], 0.0)
 
         def reduce_rows(size, partial):
-            pair_slot, _ = pack_order(listed[None, :], size)
-            pair_slot = pair_slot[0]
+            pair_slot = full_pair[0, :size]
             chosen = partial[pair_slot // owned, :, pair_slot % owned]
             share = chosen.shape[1] // pcol_size
             chosen = chosen.reshape((size, pcol_size, share) + chosen.shape[2:])
@@ -77,7 +81,6 @@
             rows = jnp.where(listed[:, None, None], -jnp.take(summed, pair_rank, axis=0), 0.0)
             return jnp.transpose(rows, (1, 0, 2))
 
-        listed = in_rows.reshape(flat_slots)
         col_factor = lax.switch(branch, [functools.partial(route, size) for size in PACKED], pieces)
         col_factor = col_factor.reshape(window, owned * local_rows, width)
         partial = jnp.einsum("wja,ij->wai", col_factor, inverse_trailing, precision=lax.Precision.HIGHEST)

time: 187 us -> 188 us (level)
  transfers between devices with their start and end apart: 3 -> 3, of which waited for: 2 -> 2; matrix products, arithmetic and copies ran while one was open for 24% -> 25% of each run, Pallas kernels for 0% -> 0%
where the time goes in v2:
time: 188 us
  blocking collectives  70.6 us (38%)
  waiting for transfers between devices  34 us (18%)
  matrix products  26.1 us (14%)
  other arithmetic  15.6 us (8%)
  local copies, waits for them, and re-layouts  14.8 us (8%)
  between operations  14.8 us (8%)
  starting transfers between devices  11.7 us (6%)
    all_gather x1, blocking collectives, shards(): pieces = lax.all_gather(mine, 'prow', axis=1, tiled=True)  37.7 us
    all_gather x1, blocking collectives, shards(): gathered = lax.all_gather(local_diag, 'prow', axis=0, tiled=False)  32.9 us
    dot_general x1, matrix products, shards(): jnp.einsum('wja,ij->wai', col_factor, inverse_trailing, precision=lax.Pre...  22.3 us
    all_to_all x1, waiting for transfers between devices, route(): received = lax.all_to_all(send, 'pcol', 0, 0, tiled=True)  17.8 us
    all_to_all x1, waiting for transfers between devices, reduce_rows(): summed = jnp.sum(lax.all_to_all(chosen, 'pcol', 1, 1, tiled=True), axis=1)  16.2 us
    all_to_all x1, starting transfers between devices, route(): received = lax.all_to_all(send, 'pcol', 0, 0, tiled=True)  7.03 us
    all_to_all x1, starting transfers between devices, reduce_rows(): summed = jnp.sum(lax.all_to_all(chosen, 'pcol', 1, 1, tiled=True), axis=1)  4.64 us
  transfers between devices with their start and end apart: 3, of which 2 were waited for; matrix products, arithmetic and copies ran while one was open for 25% of the time, Pallas kernels for 0%

profile of v2, /device:TPU:32, one launch (start us, length us, event | category | flops | bytes accessed | tf_op | source)
XLA Modules:
  0.0 187.6 jit_solution(5790671955196785404)
XLA Ops:
  7.2 0.7 compare_select_fusion.32
  8.1 1.4 gather_fusion.12
  11.2 37.7 %all_gather.12 = f32[3,256,256]{2,1,0:T(8,128)S(1)} all-gather(f32[3,16,256]{2,1,0:T(8,128)S(1)} %constant_dynamic-slice_fusion.3), channel_id=1, replica_groups=mesh['pole'=2,'prow'=16,'pcol'=16] {'prow'}, dimensions={1}, use_global_device_ids=true | all-gather | bytes 835584 | tf_op jit(solution)/shard_map/all_gather | solution.py:40
  49.6 0.8 broadcast_select_fusion.3
  51.4 1.1 compare_reduce_fusion
  52.6 1.1 iota_reduce_fusion
  53.8 1.7 gather_fusion.14
  56.3 1.3 fusion.56
  58.6 34.2 %conditional.2 = (f32[3,1024,256]{2,1,0:T(8,128)}) conditional(s32[]{:T(128)} %clamp.61, (s32[]{:T(128)}, pred[16,12]{0,1:T(8,128)(4,1)S(1)}, pred[16,12]{0,1:T(8,128)(4,1)S(1)}, s32[16,12]{0,1:T(8,128)S(1)}, s32[16,12]{0,1:T(8,128)S(1)}, /*index=5*/f32[3,16,16,256]{3,2,1,0:T(8,128)S(1)}) %tuple.87, (s32[]{:T(128)}, ...), branch_computations={%region_11.13_spmd, %region_13.15_spmd, %region_15.17_spmd} | conditional | flops 1579087 | bytes 40920736 | solution.py:84
  59.0 1.2 gather_fusion.6
  60.2 1.3 broadcast_select_fusion
  61.5 7.0 %all-to-all-start.3 = ((f32[16,6,16,256]{3,2,1,0:T(8,128)}), f32[16,6,16,256]{3,2,1,0:T(8,128)S(1)}, u32[]{:S(2)}, u32[]{:S(2)}) async-start(f32[16,6,16,256]{3,2,1,0:T(8,128)} %broadcast_select_fusion), calls=%async_computation.3 | async-start | bytes 3145728 | tf_op jit(solution)/shard_map/cond/branch_0_fun/all_to_all | solution.py:68
  69.0 17.8 %all-to-all-done.3 = f32[16,6,16,256]{3,2,1,0:T(8,128)S(1)} async-done(((f32[16,6,16,256]{3,2,1,0:T(8,128)}), f32[16,6,16,256]{3,2,1,0:T(8,128)S(1)}, u32[]{:S(2)}, u32[]{:S(2)}) %all-to-all-start.3) | async-done | bytes 1572896 | tf_op jit(solution)/shard_map/cond/branch_0_fun/all_to_all | solution.py:68
  87.0 2.5 %gather_fusion.7 = f32[12,256,256]{2,1,0:T(8,128)} fusion(f32[6,256,256]{2,1,0:T(8,128)S(1)} %bitcast.156, s32[1024]{0:T(1024)S(1)} %pad_clamp_fusion.3), kind=kCustom, calls=%fused_computation.1 | custom fusion | bytes 6291504 | tf_op jit(solution)/shard_map/cond/branch_0_fun/gather | solution.py:72
  89.4 3.4 %bitcast_select_fusion = f32[3,1024,256]{2,1,0:T(8,128)} fusion(pred[3,1024]{1,0:T(4,128)(4,1)S(1)} %bitcast.175, f32[3,1024,256]{2,1,0:T(8,128)} %bitcast.162), kind=kLoop, calls=%fused_computation.81 | loop fusion | flops 786432 | bytes 6294528 | tf_op jit(solution)/shard_map/cond/branch_0_fun/jit(_where)/select_n | solution.py:72
  92.8 1.3 and_reduce_fusion
  94.0 22.3 %fusion.48 = f32[3,256,4,256]{3,1,2,0:T(8,128)S(1)} fusion(f32[4,256,1024,1]{2,1,0,3:T(8,128)} %bitcast.171, f32[3,1024,256]{2,1,0:T(8,128)} %get-tuple-element.258), kind=kOutput, calls=%fused_computation.150 | convolution fusion | flops 9663676416 | bytes 10485760 | tf_op jit(solution)/shard_map/wja,ij->wai/dot_general | solution.py:86
  116.4 27.0 %conditional.3 = (f32[16,3,1024]{2,0,1:T(8,128)S(1)}) conditional(s32[]{:T(128)} %clamp.61, (pred[3,4]{1,0:T(4,128)(4,1)S(1)}, pred[12]{0:T(512)(128)(4,1)S(1)}, s32[1,12]{0,1:T(8,128)S(1)}, f32[3,256,4,256]{3,1,2,0:T(8,128)S(1)}) %tuple.41, (pred[3,4]{1,0:T(4,128)(4,1)S(1)}, pred[12]{0:T(512)(128)(4,1)S(1)}, ...), branch_computations={%region_17.20_spmd, %region_20.23_spmd, %region_23.26_spmd} | conditional | flops 886420 | bytes 27333400 | solution.py:88
  116.5 1.8 gather_fusion
  118.3 2.7 %copy.93 = f32[6,16,16,256]{3,2,0,1:T(8,128)} copy(f32[6,16,16,256]{3,2,1,0:T(8,128)} %bitcast.169) | data formatting | bytes 3145728 | tf_op jit(solution)/shard_map/cond/branch_0_fun/reshape | solution.py:78
  121.1 4.6 %all-to-all-start = ((f32[6,16,16,256]{3,2,0,1:T(8,128)}), f32[6,16,16,256]{3,2,0,1:T(8,128)S(1)}, u32[]{:S(2)}, u32[]{:S(2)}) async-start(f32[6,16,16,256]{3,2,0,1:T(8,128)} %copy.93), calls=%async_computation | async-start | bytes 3145728 | tf_op jit(solution)/shard_map/cond/branch_0_fun/all_to_all | solution.py:79
  126.0 16.2 %all-to-all-done = f32[6,16,16,256]{3,2,0,1:T(8,128)S(1)} async-done(((f32[6,16,16,256]{3,2,0,1:T(8,128)}), f32[6,16,16,256]{3,2,0,1:T(8,128)S(1)}, u32[]{:S(2)}, u32[]{:S(2)}) %all-to-all-start) | async-done | bytes 1572896 | tf_op jit(solution)/shard_map/cond/branch_0_fun/all_to_all | solution.py:79
  143.5 3.7 %convolution_bitcast_fusion = f32[16,3,256]{2,0,1:T(8,128)S(1)} fusion(f32[3,1024,256]{2,1,0:T(8,128)} %bitcast.172, f32[16,3,1024]{2,0,1:T(8,128)S(1)} %get-tuple-element.248), kind=kOutput, calls=%fused_computation.152 | convolution fusion | flops 150994944 | bytes 3391488 | tf_op jit(solution)/shard_map/awj,wjb->awb/dot_general | solution.py:10
  147.2 32.9 %all-gather = f32[256,3,256]{2,0,1:T(8,128)S(1)} all-gather(f32[16,3,256]{2,0,1:T(8,128)S(1)} %convolution_bitcast_fusion), channel_id=2, replica_groups=mesh['pole'=2,'prow'=16,'pcol'=16] {'prow'}, dimensions={0}, use_global_device_ids=true | all-gather | bytes 835584 | tf_op jit(solution)/shard_map/all_gather | solution.py:91
  (78 shorter events, 8.2 us)
Async XLA Ops:
  7.2 4.1 %copy-start = (f32[3,256,256]{2,1,0:T(8,128)S(1)}, f32[3,256,256]{2,1,0:T(8,128)}, u32[]{:S(2)}) copy-start(f32[3,256,256]{2,1,0:T(8,128)} %param.13) | copy-start | bytes 2359300
  7.2 136.3 %all-gather.3.cloned.1.call-start = ((), (), s32[]{:S(2)}) async-start(), calls=%async_computation.6 | async-start | bytes 3342336 | tf_op jit(solution)/shard_map/all_gather | solution.py:52
  53.8 2.5 %copy-start.5 = (s32[2]{0:T(128)S(1)}, s32[2]{0:T(128)}, u32[]{:S(2)}) copy-start(s32[2]{0:T(128)} %constant.343.clone) | copy-start | bytes 28
  61.5 25.3 %all-to-all-start.3 = ((f32[16,6,16,256]{3,2,1,0:T(8,128)}), f32[16,6,16,256]{3,2,1,0:T(8,128)S(1)}, u32[]{:S(2)}, u32[]{:S(2)}) async-start(f32[16,6,16,256]{3,2,1,0:T(8,128)} %broadcast_select_fusion), calls=%async_computation.3 | async-start | bytes 3145728 | tf_op jit(solution)/shard_map/cond/branch_0_fun/all_to_all | solution.py:68
  121.1 21.2 %all-to-all-start = ((f32[6,16,16,256]{3,2,0,1:T(8,128)}), f32[6,16,16,256]{3,2,0,1:T(8,128)S(1)}, u32[]{:S(2)}, u32[]{:S(2)}) async-start(f32[6,16,16,256]{3,2,0,1:T(8,128)} %copy.93), calls=%async_computation | async-start | bytes 3145728 | tf_op jit(solution)/shard_map/cond/branch_0_fun/all_to_all | solution.py:79
  143.4 37.4 %copy-start.3 = (f32[16,3,1024]{2,0,1:T(8,128)}, f32[16,3,1024]{2,0,1:T(8,128)S(1)}, u32[]{:S(2)}) copy-start(f32[16,3,1024]{2,0,1:T(8,128)S(1)} %get-tuple-element.248) | copy-start | bytes 589828
  143.4 36.8 %copy-start.4 = (f32[16,3,256]{2,0,1:T(8,128)S(1)}, f32[16,3,256]{2,0,1:T(8,128)}, u32[]{:S(2)}) copy-start(f32[16,3,256]{2,0,1:T(8,128)} %param.14) | copy-start | bytes 147460
  143.4 37.4 %copy-start.1 = (f32[3,256,256]{2,1,0:T(8,128)S(1)}, f32[3,256,256]{2,1,0:T(8,128)}, u32[]{:S(2)}) copy-start(f32[3,256,256]{2,1,0:T(8,128)} %param.13) | copy-start | bytes 2359300
Sparse Core Ops, SparseCore 0:
  50.5 68.4 all-gather.2

commit v3 on v2

--- a/solution.py
+++ b/solution.py
@@ -54,17 +54,16 @@
         needed = jnp.max(jnp.sum(dest_present.astype(jnp.int32), axis=1))
         branch = jnp.sum((needed > jnp.array(PACKED[:-1], jnp.int32)).astype(jnp.int32))
 
-        full_slot, full_valid = pack_order(dest_present, flat_slots)
+        full_slot, _ = pack_order(dest_present, flat_slots)
         full_j = jnp.take_along_axis(dest_index, full_slot, axis=1)
         listed = in_rows.reshape(flat_slots)
         full_pair, _ = pack_order(listed[None, :], flat_slots)
 
         def route(size, pieces):
-            send_slot, send_valid = full_slot[:, :size], full_valid[:, :size]
+            send_slot = full_slot[:, :size]
             send_w = send_slot // owned
             send_j = full_j[:, :size]
             send = pieces[send_w, send_j]
-            send = jnp.where(send_valid[..., None, None], send, 0.0)
             received = lax.all_to_all(send, "pcol", 0, 0, tiled=True)
             blocks = jnp.transpose(received, (1, 0, 2, 3)).reshape(size, local_rows, width)
             mine = dest_present[col_index]

time: 188 us -> 187 us (level)
  no operation moved by 1% of the time
where the time goes in v3:
time: 187 us
  blocking collectives  71.1 us (38%)
  waiting for transfers between devices  33.8 us (18%)
  matrix products  26.1 us (14%)
  local copies, waits for them, and re-layouts  15.8 us (8%)
  between operations  14.8 us (8%)
  other arithmetic  14 us (7%)
  starting transfers between devices  11.5 us (6%)
    all_gather x1, blocking collectives, shards(): pieces = lax.all_gather(mine, 'prow', axis=1, tiled=True)  37.7 us
    all_gather x1, blocking collectives, shards(): gathered = lax.all_gather(local_diag, 'prow', axis=0, tiled=False)  33.4 us
    dot_general x1, matrix products, shards(): jnp.einsum('wja,ij->wai', col_factor, inverse_trailing, precision=lax.Pre...  22.3 us
    all_to_all x1, waiting for transfers between devices, route(): received = lax.all_to_all(send, 'pcol', 0, 0, tiled=True)  17.9 us
    all_to_all x1, waiting for transfers between devices, reduce_rows(): summed = jnp.sum(lax.all_to_all(chosen, 'pcol', 1, 1, tiled=True), axis=1)  15.9 us
    all_to_all x1, starting transfers between devices, route(): received = lax.all_to_all(send, 'pcol', 0, 0, tiled=True)  7.03 us
    all_to_all x1, starting transfers between devices, reduce_rows(): summed = jnp.sum(lax.all_to_all(chosen, 'pcol', 1, 1, tiled=True), axis=1)  4.38 us
  transfers between devices with their start and end apart: 3, of which 2 were waited for; matrix products, arithmetic and copies ran while one was open for 25% of the time, Pallas kernels for 0%

profile of v3, /device:TPU:32, one launch (start us, length us, event | category | flops | bytes accessed | tf_op | source)
XLA Modules:
  0.0 187.1 jit_solution(11908031524303183084)
XLA Ops:
  7.2 0.7 compare_select_fusion.33
  8.1 1.4 gather_fusion.15
  10.5 0.7 compare_reduce_fusion.2
  11.3 37.7 %all_gather.12 = f32[3,256,256]{2,1,0:T(8,128)S(1)} all-gather(f32[3,16,256]{2,1,0:T(8,128)S(1)} %constant_dynamic-slice_fusion.3), channel_id=1, replica_groups=mesh['pole'=2,'prow'=16,'pcol'=16] {'prow'}, dimensions={1}, use_global_device_ids=true | all-gather | bytes 835584 | tf_op jit(solution)/shard_map/all_gather | solution.py:40
  49.6 0.8 broadcast_select_fusion
  52.1 1.3 fusion.55
  54.0 1.2 compare_reduce_fusion
  55.2 1.1 iota_reduce_fusion
  56.3 36.0 %conditional.2 = (f32[3,1024,256]{2,1,0:T(8,128)}) conditional(s32[]{:T(128)} %clamp.61, (s32[]{:T(128)}, pred[16,12]{0,1:T(8,128)(4,1)S(1)}, s32[16,12]{0,1:T(8,128)S(1)}, s32[16,3,4]{0,2,1:T(4,128)S(1)}, f32[3,16,16,256]{3,2,1,0:T(8,128)S(1)}) %tuple.86, (s32[]{:T(128)}, pred[16,12]{0,1:T(8,128)(4,1)S(1)}, ...), branch_computations={%region_10.12_spmd, %region_12.14_spmd, %region_14.16_spmd} | conditional | flops 795343 | bytes 35685240 | solution.py:83
  56.5 1.7 gather_fusion.8
  58.3 2.5 %gather_fusion.6 = f32[96,16,256]{2,1,0:T(8,128)} fusion(f32[3,16,16,256]{3,2,1,0:T(8,128)S(1)} %get-tuple-element.138, s32[96]{0:T(128)S(1)} %reshape.817), kind=kCustom, calls=%fused_computation | custom fusion | bytes 3146496 | tf_op jit(solution)/shard_map/cond/branch_0_fun/gather | solution.py:66
  60.9 7.0 %all-to-all-start.3 = ((f32[16,6,16,256]{3,2,1,0:T(8,128)}), f32[16,6,16,256]{3,2,1,0:T(8,128)S(1)}, u32[]{:S(2)}, u32[]{:S(2)}) async-start(f32[16,6,16,256]{3,2,1,0:T(8,128)} %bitcast.179), calls=%async_computation.3 | async-start | bytes 3145728 | tf_op jit(solution)/shard_map/cond/branch_0_fun/all_to_all | solution.py:67
  68.4 17.9 %all-to-all-done.3 = f32[16,6,16,256]{3,2,1,0:T(8,128)S(1)} async-done(((f32[16,6,16,256]{3,2,1,0:T(8,128)}), f32[16,6,16,256]{3,2,1,0:T(8,128)S(1)}, u32[]{:S(2)}, u32[]{:S(2)}) %all-to-all-start.3) | async-done | bytes 1572896 | tf_op jit(solution)/shard_map/cond/branch_0_fun/all_to_all | solution.py:67
  86.4 2.5 %gather_fusion.7 = f32[12,256,256]{2,1,0:T(8,128)} fusion(f32[6,256,256]{2,1,0:T(8,128)S(1)} %bitcast.166, s32[1024]{0:T(1024)S(1)} %pad_clamp_fusion.3), kind=kCustom, calls=%fused_computation.1 | custom fusion | bytes 6291504 | tf_op jit(solution)/shard_map/cond/branch_0_fun/gather | solution.py:71
  88.9 3.4 %bitcast_select_fusion = f32[3,1024,256]{2,1,0:T(8,128)} fusion(pred[3,1024]{1,0:T(4,128)(4,1)S(1)} %bitcast.185, f32[3,1024,256]{2,1,0:T(8,128)} %bitcast.172), kind=kLoop, calls=%fused_computation.83 | loop fusion | flops 786432 | bytes 6294528 | tf_op jit(solution)/shard_map/cond/branch_0_fun/jit(_where)/select_n | solution.py:71
  92.3 1.3 and_reduce_fusion
  93.5 22.3 %fusion.48 = f32[3,256,4,256]{3,1,2,0:T(8,128)S(1)} fusion(f32[4,256,1024,1]{2,1,0,3:T(8,128)} %bitcast.181, f32[3,1024,256]{2,1,0:T(8,128)} %get-tuple-element.292), kind=kOutput, calls=%fused_computation.157 | convolution fusion | flops 9663676416 | bytes 10485760 | tf_op jit(solution)/shard_map/wja,ij->wai/dot_general | solution.py:85
  115.9 26.4 %conditional.3 = (f32[16,3,1024]{2,0,1:T(8,128)S(1)}) conditional(s32[]{:T(128)} %clamp.61, (pred[3,4]{1,0:T(4,128)(4,1)S(1)}, pred[12]{0:T(512)(128)(4,1)S(1)}, s32[1,12]{0,1:T(8,128)S(1)}, f32[3,256,4,256]{3,1,2,0:T(8,128)S(1)}) %tuple.44, (pred[3,4]{1,0:T(4,128)(4,1)S(1)}, pred[12]{0:T(512)(128)(4,1)S(1)}, ...), branch_computations={%region_16.19_spmd, %region_19.22_spmd, %region_22.25_spmd} | conditional | flops 886420 | bytes 27333400 | solution.py:87
  116.0 1.8 gather_fusion
  117.8 2.7 %copy.71 = f32[6,16,16,256]{3,2,0,1:T(8,128)} copy(f32[6,16,16,256]{3,2,1,0:T(8,128)} %bitcast.180) | data formatting | bytes 3145728 | tf_op jit(solution)/shard_map/cond/branch_0_fun/reshape | solution.py:77
  120.6 4.4 %all-to-all-start = ((f32[6,16,16,256]{3,2,0,1:T(8,128)}), f32[6,16,16,256]{3,2,0,1:T(8,128)S(1)}, u32[]{:S(2)}, u32[]{:S(2)}) async-start(f32[6,16,16,256]{3,2,0,1:T(8,128)} %copy.71), calls=%async_computation | async-start | bytes 3145728 | tf_op jit(solution)/shard_map/cond/branch_0_fun/all_to_all | solution.py:78
  125.3 15.9 %all-to-all-done = f32[6,16,16,256]{3,2,0,1:T(8,128)S(1)} async-done(((f32[6,16,16,256]{3,2,0,1:T(8,128)}), f32[6,16,16,256]{3,2,0,1:T(8,128)S(1)}, u32[]{:S(2)}, u32[]{:S(2)}) %all-to-all-start) | async-done | bytes 1572896 | tf_op jit(solution)/shard_map/cond/branch_0_fun/all_to_all | solution.py:78
  142.4 3.7 %convolution_bitcast_fusion = f32[16,3,256]{2,0,1:T(8,128)S(1)} fusion(f32[3,1024,256]{2,1,0:T(8,128)} %bitcast.182, f32[16,3,1024]{2,0,1:T(8,128)S(1)} %get-tuple-element.282), kind=kOutput, calls=%fused_computation.159 | convolution fusion | flops 150994944 | bytes 3391488 | tf_op jit(solution)/shard_map/awj,wjb->awb/dot_general | solution.py:10
  146.1 33.4 %all-gather = f32[256,3,256]{2,0,1:T(8,128)S(1)} all-gather(f32[16,3,256]{2,0,1:T(8,128)S(1)} %convolution_bitcast_fusion), channel_id=2, replica_groups=mesh['pole'=2,'prow'=16,'pcol'=16] {'prow'}, dimensions={0}, use_global_device_ids=true | all-gather | bytes 835584 | tf_op jit(solution)/shard_map/all_gather | solution.py:90
  (72 shorter events, 6.8 us)
Async XLA Ops:
  7.2 4.1 %copy-start = (f32[3,256,256]{2,1,0:T(8,128)S(1)}, f32[3,256,256]{2,1,0:T(8,128)}, u32[]{:S(2)}) copy-start(f32[3,256,256]{2,1,0:T(8,128)} %param.13) | copy-start | bytes 2359300
  7.2 44.9 %copy-start.5 = (s32[2]{0:T(128)S(1)}, s32[2]{0:T(128)}, u32[]{:S(2)}) copy-start(s32[2]{0:T(128)} %constant.357.clone) | copy-start | bytes 28
  7.2 135.2 %all-gather.3.cloned.1.call-start = ((), (), s32[]{:S(2)}) async-start(), calls=%async_computation.6 | async-start | bytes 3342336 | tf_op jit(solution)/shard_map/all_gather | solution.py:52
  60.9 25.4 %all-to-all-start.3 = ((f32[16,6,16,256]{3,2,1,0:T(8,128)}), f32[16,6,16,256]{3,2,1,0:T(8,128)S(1)}, u32[]{:S(2)}, u32[]{:S(2)}) async-start(f32[16,6,16,256]{3,2,1,0:T(8,128)} %bitcast.179), calls=%async_computation.3 | async-start | bytes 3145728 | tf_op jit(solution)/shard_map/cond/branch_0_fun/all_to_all | solution.py:67
  120.6 20.6 %all-to-all-start = ((f32[6,16,16,256]{3,2,0,1:T(8,128)}), f32[6,16,16,256]{3,2,0,1:T(8,128)S(1)}, u32[]{:S(2)}, u32[]{:S(2)}) async-start(f32[6,16,16,256]{3,2,0,1:T(8,128)} %copy.71), calls=%async_computation | async-start | bytes 3145728 | tf_op jit(solution)/shard_map/cond/branch_0_fun/all_to_all | solution.py:78
  142.3 37.9 %copy-start.3 = (f32[16,3,1024]{2,0,1:T(8,128)}, f32[16,3,1024]{2,0,1:T(8,128)S(1)}, u32[]{:S(2)}) copy-start(f32[16,3,1024]{2,0,1:T(8,128)S(1)} %get-tuple-element.282) | copy-start | bytes 589828
  142.3 37.3 %copy-start.4 = (f32[16,3,256]{2,0,1:T(8,128)S(1)}, f32[16,3,256]{2,0,1:T(8,128)}, u32[]{:S(2)}) copy-start(f32[16,3,256]{2,0,1:T(8,128)} %param.14) | copy-start | bytes 147460
  142.3 37.9 %copy-start.1 = (f32[3,256,256]{2,1,0:T(8,128)S(1)}, f32[3,256,256]{2,1,0:T(8,128)}, u32[]{:S(2)}) copy-start(f32[3,256,256]{2,1,0:T(8,128)} %param.13) | copy-start | bytes 2359300
Sparse Core Ops, SparseCore 0:
  50.6 67.8 all-gather.2
